TPU v7x, 512 devices: a whole 4x8x8 slice. The times are simulated.
512 devices in a mesh: rep: 8 (over y_hi, core), tp: 64 (over x, z, y_lo).
Axes of the slice: x: 4, y: 8 (y_hi: 4, y_lo: 2; y = y_hi * 2 + y_lo), z: 8, core: 2. Of those that a mesh axis runs over, the one named last changes fastest.
Arguments:
- tokens: bfloat16 [4096, 6144], P(('rep', 'tp')), parts along dimension 0, may hold values from -6 to 6
- ln_gain: bfloat16 [6144], replicated, may hold values from 0.5 to 1.5
- ln_bias: bfloat16 [6144], replicated, may hold values from -4 to 4
- w_qkv: bfloat16 [6144, 18432], P(None, 'tp'), may hold values from -0.078125 to 0.078125
- b_qkv: bfloat16 [18432], P('tp'), may hold values from -6 to 6
- w_dense: bfloat16 [6144, 6144], P(None, 'tp'), may hold values from -0.625 to 0.625
- b_dense: bfloat16 [6144], replicated, may hold values from -6 to 6
- prefix_kv: bfloat16 [2, 32, 128, 6144], P(None, 'rep', None, 'tp'), parts along dimension 1, may hold values from -110 to 110
- decode_kv: bfloat16 [2, 256, 16, 6144], P(None, 'rep', None, 'tp'), parts along dimension 1, may hold values from -110 to 110
- prefix_lens: int32 [32], P('rep'), parts along dimension 0, may hold values from 0 to 128, as said below
- span_request: int32 [32], P('rep'), parts along dimension 0, may hold values from 0 to 3, each once
- decode_lens: int32 [256], P('rep'), parts along dimension 0, may hold values from 1 to 16, 256 in all
- slot_valid: int32 [256, 16], P('rep'), parts along dimension 0, may hold values 0 or 1
Outputs:
- layer_out: bfloat16 [4096, 6144], P(('rep', 'tp')), parts along dimension 0
There are 8 independent parts, one for each index of `rep`. A program takes and returns all parts, laid end to end along the dimension named above; an argument that names none is the same for every part. Nothing has to cross between parts.
Inputs may be any that keep to these rules, and one draw needn't show every extreme that they name: `prefix_lens`: some request slot has exactly 128 cached tokens. `span_request`: each request slot is continued by exactly one span. `decode_lens`: the lengths sum to 256 and one equals 16.
All inputs are finite; a program needn't handle non-finite values.
Results may differ from a plain program's by a relative error of at most 0.012.
The roundings to bfloat16 on the way count: a program that leaves them out, or rounds other values in their place, can miss the bound.
Values may be sent and summed in bfloat16 or wider, within the bound.
No kernel may reach another device: no remote copies, remote signals or barrier semaphores. Data moves between devices by JAX's collectives and lax.ppermute only.
A program may use at most 64 MiB of HBM per device.

v0:
```python
import math
import jax
import jax.numpy as jnp
from jax import lax
from jax.sharding import PartitionSpec as P

ROT = 24


def layer_norm(rows, gain, shift):
    value_matrix = rows.astype(jnp.float32)
    center = value_matrix - jnp.mean(value_matrix, axis=-1, keepdims=True)
    spread = jnp.mean(center * center, axis=-1, keepdims=True)
    scaled = center * lax.rsqrt(spread + 1e-05)
    return (scaled * gain.astype(jnp.float32) + shift.astype(jnp.float32)).astype(jnp.bfloat16)


def rotary_tables(places, rot_dims):
    counter = jnp.arange(rot_dims // 2, dtype=jnp.float32)
    inverse = jnp.exp(counter * (-2.0 * math.log(10000.0) / rot_dims))
    angles = places.astype(jnp.float32)[:, None] * inverse[None, :]
    return (jnp.cos(angles), jnp.sin(angles))


def rotate(field, cosine, sine):
    half = cosine.shape[-1]
    first = field[..., :half]
    second = field[..., half : 2 * half]
    return jnp.concatenate(
        [first * cosine - second * sine, second * cosine + first * sine, field[..., 2 * half :]],
        axis=-1,
    )


def token_places(span_lens, cache_lens, span_rows):
    within = jnp.arange(span_rows, dtype=jnp.int32)
    prefill = (span_lens[:, None] + within[None, :]).reshape(-1)
    return jnp.concatenate([prefill, cache_lens])


def batch_stacked(form, left, right):
    return jnp.einsum(form, left, right, preferred_element_type=jnp.float32)


def attend(logit_scores, live, value_matrix):
    peaks = jnp.max(jnp.where(live, logit_scores, -1e30), axis=-1, keepdims=True)
    raised = jnp.where(live, jnp.exp(logit_scores - peaks), 0.0)
    softmax_weights = (raised / jnp.sum(raised, axis=-1, keepdims=True)).astype(jnp.bfloat16)
    return batch_stacked("lsw,lwe->lse", softmax_weights, value_matrix).astype(jnp.bfloat16)


def prefill_attention(
    query, keys, value_matrix, prefix_keys, prefix_vals, span_lens, decode_rows, score_scale
):
    spans = prefix_keys.shape[0]
    slots = prefix_keys.shape[1]
    span_rows = (query.shape[0] - decode_rows) // spans
    prefill_rows = spans * span_rows
    head = query.shape[-1]
    prefill_query_span = query[:prefill_rows].reshape(spans, span_rows, head)
    combined_key_rows = jnp.concatenate(
        [prefix_keys, keys[:prefill_rows].reshape(spans, span_rows, head)], axis=1
    )
    all_vals = jnp.concatenate(
        [prefix_vals, value_matrix[:prefill_rows].reshape(spans, span_rows, head)], axis=1
    )
    logit_scores = (
        batch_stacked("jrf,jyf->jry", prefill_query_span, combined_key_rows) * score_scale
    )
    column = jnp.arange(slots + span_rows, dtype=jnp.int32)[None, None, :]
    row_index = jnp.arange(span_rows, dtype=jnp.int32)[None, :, None]
    live = jnp.where(column < slots, column < span_lens[:, None, None], column - slots <= row_index)
    return attend(logit_scores, live, all_vals).reshape(prefill_rows, head)


def decode_attention(
    query, keys, value_matrix, stored_key_cache, cache_vals, cache_lens, slot_valid, score_scale
):
    decode_rows = stored_key_cache.shape[0]
    slots = stored_key_cache.shape[1]
    first_row = query.shape[0] - decode_rows
    decode_query_row = query[first_row:]
    own_keys = keys[first_row:]
    own_vals = value_matrix[first_row:]
    cache_present = (
        batch_stacked("jrf,jyf->jry", decode_query_row[:, None, :], stored_key_cache) * score_scale
    )
    itself = (
        jnp.sum(decode_query_row.astype(jnp.float32) * own_keys.astype(jnp.float32), axis=-1)[
            :, None, None
        ]
        * score_scale
    )
    logit_scores = jnp.concatenate([cache_present, itself], axis=-1)
    column = jnp.arange(slots, dtype=jnp.int32)[None, :]
    live_cache = (column < cache_lens[:, None]) & (slot_valid == 1)
    live = jnp.concatenate([live_cache, jnp.ones((decode_rows, 1), dtype=bool)], axis=-1)[
        :, None, :
    ]
    all_vals = jnp.concatenate([cache_vals, own_vals[:, None, :]], axis=1)
    return attend(logit_scores, live, all_vals)[:, 0, :]


def on_device(
    tokens,
    ln_gain,
    ln_bias,
    w_qkv,
    b_qkv,
    w_dense,
    b_dense,
    prefix_kv,
    decode_kv,
    prefix_lens,
    span_request,
    decode_lens,
    slot_valid,
):
    normed = layer_norm(tokens, ln_gain, ln_bias)
    joined = jnp.dot(
        lax.all_gather(normed, "tp", axis=0, tiled=True), w_qkv, preferred_element_type=jnp.float32
    )
    joined = joined + b_qkv.astype(jnp.float32)
    head = joined.shape[1] // 3
    token_count = joined.shape[0]
    spans = prefix_kv.shape[1]
    decode_rows = decode_kv.shape[1]
    span_rows = (token_count - decode_rows) // spans
    span_lens = jnp.take(prefix_lens, span_request, axis=0)
    cosine, sine = rotary_tables(token_places(span_lens, decode_lens, span_rows), ROT)
    query = rotate(joined[:, :head], cosine, sine).astype(jnp.bfloat16)
    keys = rotate(joined[:, head : 2 * head], cosine, sine).astype(jnp.bfloat16)
    value_matrix = joined[:, 2 * head :].astype(jnp.bfloat16)
    prefix_keys = jnp.take(prefix_kv[0], span_request, axis=0)
    prefix_vals = jnp.take(prefix_kv[1], span_request, axis=0)
    score_scale = 1.0 / math.sqrt(head)
    early = prefill_attention(
        query, keys, value_matrix, prefix_keys, prefix_vals, span_lens, decode_rows, score_scale
    )
    late = decode_attention(
        query, keys, value_matrix, decode_kv[0], decode_kv[1], decode_lens, slot_valid, score_scale
    )
    heads_out = jnp.concatenate([early, late], axis=0)
    mixed = jnp.dot(
        lax.all_gather(heads_out, "tp", axis=1, tiled=True),
        w_dense,
        preferred_element_type=jnp.float32,
    )
    own_rows = lax.all_to_all(mixed, "tp", split_axis=0, concat_axis=1, tiled=True)
    attn = (own_rows + b_dense.astype(jnp.float32)).astype(jnp.bfloat16)
    return (attn.astype(jnp.float32) + tokens.astype(jnp.float32)).astype(jnp.bfloat16)


def solution(mesh):
    placed = (
        P(("rep", "tp"), None),
        P(),
        P(),
        P(None, "tp"),
        P("tp"),
        P(None, "tp"),
        P(),
        P(None, "rep", None, "tp"),
        P(None, "rep", None, "tp"),
        P("rep"),
        P("rep"),
        P("rep"),
        P("rep", None),
    )
    return jax.shard_map(
        on_device, mesh=mesh, in_specs=placed, out_specs=P(("rep", "tp"), None), check_vma=False
    )
```

profile of v0, /device:TPU:8, one launch (start us, length us, event | category | flops | bytes accessed | tf_op | source)
XLA Modules:
  0.0 731.0 jit_solution(18445028543384354713)
XLA Ops:
  10.5 1.6 fusion.15
  16.8 1.6 slice_bitcast_fusion.1
  18.5 2.1 gather_fusion.2
  20.5 2.1 gather_fusion.1
  27.7 1.6 slice_bitcast_fusion
  29.3 1.7 broadcast_select_fusion
  31.0 305.6 %all-gather.3.cloned.1.call-done = bf16[512,6144]{1,0:T(8,128)(2,1)} async-done(((bf16[8,6144]{1,0:T(8,128)(2,1)}), bf16[512,6144]{1,0:T(8,128)(2,1)}) %all-gather.3.cloned.1.call-update) | async-done | bytes 6291472 | tf_op jit(solution)/shard_map/all_gather | solution.py:121
  336.5 4.8 fusion.55
  353.7 1.7 multiply_reduce_fusion
  356.8 1.6 reshape.178
  358.4 1.5 copy.25
  360.0 1.6 reshape.177
  361.6 1.6 reshape.179
  368.0 2.9 convolution_convert_fusion
  370.9 1.6 copy.28
  372.4 1.7 reshape.180
  374.1 1.6 pad_maximum_fusion.2
  375.7 317.5 %all-gather.5.cloned.1.call-done = bf16[512,6144]{0,1:T(8,128)(2,1)} async-done(((bf16[512,96]{0,1:T(8,128)(2,1)}), bf16[512,6144]{0,1:T(8,128)(2,1)}) %all-gather.5.cloned.1.call-update) | async-done | bytes 6291472 | tf_op jit(solution)/shard_map/all_gather | solution.py:145
  693.3 5.6 convolution_bitcast_fusion
  698.9 9.1 %all-to-all-start = ((f32[64,8,96]{2,1,0:T(8,128)}), f32[64,8,96]{2,1,0:T(8,128)}, u32[]{:S(2)}, u32[]{:S(2)}) async-start(f32[64,8,96]{2,1,0:T(8,128)} %convolution_bitcast_fusion), calls=%async_computation | async-start | bytes 524288 | tf_op jit(solution)/shard_map/all_to_all | solution.py:149
  708.6 10.4 %all-to-all-done = f32[64,8,96]{2,1,0:T(8,128)} async-done(((f32[64,8,96]{2,1,0:T(8,128)}), f32[64,8,96]{2,1,0:T(8,128)}, u32[]{:S(2)}, u32[]{:S(2)}) %all-to-all-start) | async-done | bytes 196640 | tf_op jit(solution)/shard_map/all_to_all | solution.py:149
  719.0 1.7 copy.31
  720.7 1.8 all_to_all.17
  722.5 1.7 fusion.16
  (55 shorter events, 32.7 us)
Async XLA Ops:
  6.5 330.0 %copy-start = (bf16[6144,288]{0,1:T(8,128)(2,1)S(1)}, bf16[6144,288]{0,1:T(8,128)(2,1)}, u32[]{:S(2)}) copy-start(bf16[6144,288]{0,1:T(8,128)(2,1)} %param.18) | copy-start | bytes 10616836
  6.5 330.0 %all-gather.3.cloned.1.call-start = ((), (), s32[]{:S(2)}) async-start(), calls=%async_computation.1 | async-start | bytes 6389760 | tf_op jit(solution)/shard_map/all_gather | solution.py:121
  12.2 681.1 %all-gather.5.cloned.1.call-start = ((), (), s32[]{:S(2)}) async-start(), calls=%async_computation.2 | async-start | bytes 6389760 | tf_op jit(solution)/shard_map/all_gather | solution.py:145
  16.1 0.6 copy-start.3
  31.0 311.1 %copy-start.4 = (f32[12]{0:T(128)S(1)}, f32[12]{0:T(128)}, u32[]{:S(2)}) copy-start(f32[12]{0:T(128)} %multiply_exponential_fusion) | copy-start | bytes 148
  366.1 0.8 copy-start.1
  367.9 340.0 %copy-start.2 = (bf16[6144]{0:T(1024)(128)(2,1)S(1)}, bf16[6144]{0:T(1024)(128)(2,1)}, u32[]{:S(2)}) copy-start(bf16[6144]{0:T(1024)(128)(2,1)} %param.21) | copy-start | bytes 36868
  698.9 20.1 %all-to-all-start = ((f32[64,8,96]{2,1,0:T(8,128)}), f32[64,8,96]{2,1,0:T(8,128)}, u32[]{:S(2)}, u32[]{:S(2)}) async-start(f32[64,8,96]{2,1,0:T(8,128)} %convolution_bitcast_fusion), calls=%async_computation | async-start | bytes 524288 | tf_op jit(solution)/shard_map/all_to_all | solution.py:149
Sparse Core Ops, SparseCore 0:
  12.3 324.1 all-gather.2
  375.9 317.3 all-gather.4
where the time goes:
time: 732 us; the launch traced here: 731 us
  waiting for transfers between devices  634 us (87%)
  local copies, waits for them, and re-layouts  31.8 us (4%)
  other arithmetic  28.4 us (4%)
  matrix products  14.6 us (2%)
  between operations  13.5 us (2%)
  starting transfers between devices  9.13 us (1%)
    all_gather x1, waiting for transfers between devices, on_device(): lax.all_gather(heads_out, 'tp', axis=1, tiled=True)  318 us
    all_gather x1, waiting for transfers between devices, on_device(): lax.all_gather(normed, 'tp', axis=0, tiled=True)  306 us
  transfers between devices with their start and end apart: 3, of which 3 were waited for; matrix products, arithmetic and copies ran while one was open for 3% of the time, Pallas kernels for 0%

commit v1 on v0

--- a/solution.py
+++ b/solution.py
@@ -118,7 +118,11 @@
 ):
     normed = layer_norm(tokens, ln_gain, ln_bias)
     joined = jnp.dot(
-        lax.all_gather(normed, "tp", axis=0, tiled=True), w_qkv, preferred_element_type=jnp.float32
+        jnp.concatenate(
+            lax.all_to_all(jnp.stack([normed] * lax.axis_size("tp")), "tp", 0, 0), axis=0
+        ),
+        w_qkv,
+        preferred_element_type=jnp.float32,
     )
     joined = joined + b_qkv.astype(jnp.float32)
     head = joined.shape[1] // 3

time: 732 us -> 572 us (0.78)
  waiting for transfers between devices: 634 us -> 456 us
  starting transfers between devices: 9.13 us -> 24.2 us
    all_gather x1 -> x0, waiting for transfers between devices: 306 us -> none  [on_device(): lax.all_gather(normed, 'tp', axis=0, tiled=True)]
    all_to_all x0 -> x1, waiting for transfers between devices: none -> 128 us  [on_device(): lax.all_to_all(jnp.stack([normed] * lax.axis_size('tp')), 'tp', 0, 0)]
    all_to_all x0 -> x1, starting transfers between devices: none -> 15.1 us  [on_device(): lax.all_to_all(jnp.stack([normed] * lax.axis_size('tp')), 'tp', 0, 0)]
where the time goes in v1:
time: 572 us; the launch traced here: 571 us
  waiting for transfers between devices  456 us (80%)
  local copies, waits for them, and re-layouts  35.4 us (6%)
  other arithmetic  27.4 us (5%)
  starting transfers between devices  24.2 us (4%)
  matrix products  14.6 us (3%)
  between operations  13.5 us (2%)
    all_gather x1, waiting for transfers between devices, on_device(): lax.all_gather(heads_out, 'tp', axis=1, tiled=True)  317 us
    all_to_all x1, waiting for transfers between devices, on_device(): lax.all_to_all(jnp.stack([normed] * lax.axis_size('tp')), 'tp', 0, 0)  128 us
    all_to_all x1, starting transfers between devices, on_device(): lax.all_to_all(jnp.stack([normed] * lax.axis_size('tp')), 'tp', 0, 0)  15.1 us
  transfers between devices with their start and end apart: 3, of which 3 were waited for; matrix products, arithmetic and copies ran while one was open for 3% of the time, Pallas kernels for 0%

profile of v1, /device:TPU:8, one launch (start us, length us, event | category | flops | bytes accessed | tf_op | source)
XLA Modules:
  0.0 570.6 jit_solution(8564756677092287265)
XLA Ops:
  11.5 3.4 stack.2
  14.9 15.1 %all-to-all-start = ((bf16[64,8,6144]{2,1,0:T(8,128)(2,1)}), bf16[64,8,6144]{2,1,0:T(8,128)(2,1)}, u32[]{:S(2)}, u32[]{:S(2)}) async-start(bf16[64,8,6144]{2,1,0:T(8,128)(2,1)} %stack.2), calls=%async_computation | async-start | bytes 12582912 | tf_op jit(solution)/shard_map/all_to_all | solution.py:122
  34.4 1.6 slice_bitcast_fusion.1
  36.0 2.2 gather_fusion.2
  38.2 2.2 gather_fusion.1
  45.4 1.6 slice_bitcast_fusion
  47.0 1.7 broadcast_select_fusion
  48.7 127.9 %all-to-all-done = bf16[64,8,6144]{2,1,0:T(8,128)(2,1)} async-done(((bf16[64,8,6144]{2,1,0:T(8,128)(2,1)}), bf16[64,8,6144]{2,1,0:T(8,128)(2,1)}, u32[]{:S(2)}, u32[]{:S(2)}) %all-to-all-start) | async-done | bytes 6291488 | tf_op jit(solution)/shard_map/all_to_all | solution.py:122
  176.6 4.8 fusion.60
  193.7 1.7 multiply_reduce_fusion
  196.8 1.6 reshape.184
  200.0 1.6 reshape.183
  201.7 1.6 reshape.185
  208.0 2.9 convolution_convert_fusion
  210.9 1.6 copy.28
  212.5 1.7 reshape.186
  214.1 1.6 pad_maximum_fusion.2
  215.8 317.1 %all-gather.2.cloned.1.call-done = bf16[512,6144]{0,1:T(8,128)(2,1)} async-done(((bf16[512,96]{0,1:T(8,128)(2,1)}), bf16[512,6144]{0,1:T(8,128)(2,1)}) %all-gather.2.cloned.1.call-update) | async-done | bytes 6291472 | tf_op jit(solution)/shard_map/all_gather | solution.py:149
  532.9 5.6 convolution_bitcast_fusion
  538.5 9.1 %all-to-all-start.1 = ((f32[64,8,96]{2,1,0:T(8,128)}), f32[64,8,96]{2,1,0:T(8,128)}, u32[]{:S(2)}, u32[]{:S(2)}) async-start(f32[64,8,96]{2,1,0:T(8,128)} %convolution_bitcast_fusion), calls=%async_computation.1 | async-start | bytes 524288 | tf_op jit(solution)/shard_map/all_to_all | solution.py:153
  548.2 10.4 %all-to-all-done.1 = f32[64,8,96]{2,1,0:T(8,128)} async-done(((f32[64,8,96]{2,1,0:T(8,128)}), f32[64,8,96]{2,1,0:T(8,128)}, u32[]{:S(2)}, u32[]{:S(2)}) %all-to-all-start.1) | async-done | bytes 196640 | tf_op jit(solution)/shard_map/all_to_all | solution.py:153
  558.7 1.7 copy.31
  560.4 1.8 all_to_all.21
  562.1 1.7 fusion.21
  (63 shorter events, 34.8 us)
Async XLA Ops:
  6.5 170.1 %copy-start = (bf16[6144,288]{0,1:T(8,128)(2,1)S(1)}, bf16[6144,288]{0,1:T(8,128)(2,1)}, u32[]{:S(2)}) copy-start(bf16[6144,288]{0,1:T(8,128)(2,1)} %param.18) | copy-start | bytes 10616836
  14.9 15.2 %copy-start.7 = (bf16[288]{0:T(512)(128)(2,1)S(1)}, bf16[288]{0:T(512)(128)(2,1)}, u32[]{:S(2)}) copy-start(bf16[288]{0:T(512)(128)(2,1)} %param.19) | copy-start | bytes 1732
  14.9 16.4 %copy-start.1 = (s32[4]{0:T(128)S(1)}, s32[4]{0:T(128)}, u32[]{:S(2)}) copy-start(s32[4]{0:T(128)} %param.24) | copy-start | bytes 52
  14.9 28.7 %copy-start.4 = (s32[32,16]{0,1:T(8,128)S(1)}, s32[32,16]{0,1:T(8,128)}, u32[]{:S(2)}) copy-start(s32[32,16]{0,1:T(8,128)} %param.27) | copy-start | bytes 6148
  14.9 161.7 %all-to-all-start = ((bf16[64,8,6144]{2,1,0:T(8,128)(2,1)}), bf16[64,8,6144]{2,1,0:T(8,128)(2,1)}, u32[]{:S(2)}, u32[]{:S(2)}) async-start(bf16[64,8,6144]{2,1,0:T(8,128)(2,1)} %stack.2), calls=%async_computation | async-start | bytes 12582912 | tf_op jit(solution)/shard_map/all_to_all | solution.py:122
  30.0 502.9 %all-gather.2.cloned.1.call-start = ((), (), s32[]{:S(2)}) async-start(), calls=%async_computation.2 | async-start | bytes 6389760 | tf_op jit(solution)/shard_map/all_gather | solution.py:149
  31.3 2.3 copy-start.5
  33.6 0.6 copy-start.6
  48.7 133.5 %copy-start.8 = (f32[12]{0:T(128)S(1)}, f32[12]{0:T(128)}, u32[]{:S(2)}) copy-start(f32[12]{0:T(128)} %multiply_exponential_fusion) | copy-start | bytes 148
  206.1 0.8 copy-start.2
  208.0 339.6 %copy-start.3 = (bf16[6144]{0:T(1024)(128)(2,1)S(1)}, bf16[6144]{0:T(1024)(128)(2,1)}, u32[]{:S(2)}) copy-start(bf16[6144]{0:T(1024)(128)(2,1)} %param.21) | copy-start | bytes 36868
  538.5 20.1 %all-to-all-start.1 = ((f32[64,8,96]{2,1,0:T(8,128)}), f32[64,8,96]{2,1,0:T(8,128)}, u32[]{:S(2)}, u32[]{:S(2)}) async-start(f32[64,8,96]{2,1,0:T(8,128)} %convolution_bitcast_fusion), calls=%async_computation.1 | async-start | bytes 524288 | tf_op jit(solution)/shard_map/all_to_all | solution.py:153
Sparse Core Ops, SparseCore 0:
  215.9 316.9 all-gather.1
